TPU v7x, 32 devices: a whole 2x2x4 slice. The times are simulated.
32 devices in a mesh: dp: 8 (over z, x), tensor: 4 (over y, core).
Axes of the slice: x: 2, y: 2, z: 4, core: 2. Of those that a mesh axis runs over, the one named last changes fastest.
Arguments:
- hidden: bfloat16 [16384, 1024], P('dp'), may hold values from -6 to 6
- lengths: int32 [8], P('dp'), may hold values from 1365 to 2048, as said below
- norm_gain: float32 [1024], replicated, may hold values from 0.1 to 1.9
- z_weight: bfloat16 [1024, 2048], P(None, 'tensor'), may hold values from -0.1875 to 0.1875
- x_weight: bfloat16 [1024, 2048], P(None, 'tensor'), may hold values from -0.1875 to 0.1875
- bc_weight: bfloat16 [1024, 256], replicated, may hold values from -0.1875 to 0.1875
- dt_weight: bfloat16 [1024, 32], P(None, 'tensor'), may hold values from -0.1875 to 0.1875
- x_kernel: float32 [4, 2048], P(None, 'tensor'), may hold values from -3 to 3
- bc_kernel: float32 [4, 256], replicated, may hold values from -3 to 3
- x_offset: float32 [2048], P('tensor'), may hold values from -3 to 3
- bc_offset: float32 [256], replicated, may hold values from -3 to 3
- step_bias: float32 [32], P('tensor'), may hold values from -5 to -1
- decay_log: float32 [32], P('tensor'), may hold values from 0 to 2.5
- skip_gain: float32 [32], P('tensor'), may hold values from 0.5 to 1.5
- gate_gain: float32 [2048], P('tensor'), may hold values from 0.1 to 1.9
- out_weight: bfloat16 [2048, 1024], P('tensor'), may hold values from -0.125 to 0.125
- cotangent: bfloat16 [16384, 1024], P('dp'), may hold values from -6 to 6
Outputs:
- output: bfloat16 [16384, 1024], P('dp')
- grad_hidden: float32 [16384, 1024], P('dp')
- grad_norm_gain: float32 [1024], replicated
- grad_z_weight: float32 [1024, 2048], P(None, 'tensor')
- grad_x_weight: float32 [1024, 2048], P(None, 'tensor')
- grad_bc_weight: float32 [1024, 256], replicated
- grad_dt_weight: float32 [1024, 32], P(None, 'tensor')
- grad_x_kernel: float32 [4, 2048], P(None, 'tensor')
- grad_bc_kernel: float32 [4, 256], replicated
- grad_x_offset: float32 [2048], P('tensor')
- grad_bc_offset: float32 [256], replicated
- grad_step_bias: float32 [32], P('tensor')
- grad_decay_log: float32 [32], P('tensor')
- grad_skip_gain: float32 [32], P('tensor')
- grad_gate_gain: float32 [2048], P('tensor')
- grad_out_weight: float32 [2048, 1024], P('tensor')
Inputs may be any that keep to these rules, and one draw needn't show every extreme that they name: `lengths`: each slot's sequence length; some slot has exactly 2048 in every draw.
All inputs are finite; a program needn't handle non-finite values.
Results may differ from a plain program's by a relative error of at most 0.0096.
Values may be sent and summed in bfloat16 or wider, within the bound.
No kernel may reach another device: no remote copies, remote signals or barrier semaphores. Data moves between devices by JAX's collectives and lax.ppermute only.
A program may use at most 192 MiB of HBM per device.

v0:
```python
import jax
import jax.numpy as jnp
from jax import lax
from jax.sharding import PartitionSpec as P

CH = 256
DI = 2048
precise = lax.Precision.HIGHEST
epsilon = 1e-05


def causal_conv(signal, kernel, offset):
    taps = kernel.shape[0]
    length = signal.shape[0]
    padded = jnp.pad(signal, ((taps - 1, 0), (0, 0)))
    total = jnp.zeros_like(signal) + offset[None, :]
    for tap_index in range(taps):
        total = total + kernel[tap_index][None, :] * padded[tap_index : tap_index + length]
    return total


def conv_act(signal, kernel, offset):
    return jax.nn.silu(causal_conv(signal, kernel, offset))


def group_step(carry_state, block_in):
    values, log_rates, b_rows, c_rows = block_in
    block_len = log_rates.shape[1]
    causal_mask = lax.broadcasted_iota(
        jnp.int32, (block_len, block_len), 0
    ) >= lax.broadcasted_iota(jnp.int32, (block_len, block_len), 1)
    summed = jnp.cumsum(log_rates, axis=1)
    spread = summed[:, :, None] - summed[:, None, :]
    decays = jnp.exp(jnp.where(causal_mask[None], spread, -1e30))
    scores = jnp.dot(c_rows, b_rows.T, precision=precise, preferred_element_type=jnp.float32)
    within = jnp.einsum("hts,hsp->htp", scores[None] * decays, values, precision=precise)
    carried = (
        jnp.einsum("tn,hnp->htp", c_rows, carry_state, precision=precise)
        * jnp.exp(summed)[:, :, None]
    )
    remain = jnp.exp(summed[:, -1:] - summed)
    updated = carry_state * jnp.exp(summed[:, -1])[:, None, None] + jnp.einsum(
        "sn,hsp->hnp", b_rows, values * remain[:, :, None], precision=precise
    )
    return (updated, within + carried)


def mixer(conv_vals, state_vals, step_raw, step_bias, decay_log, skip_gain, live_mask):
    row_count, channels = conv_vals.shape
    head_count = step_raw.shape[1]
    head_size = channels // head_count
    state_size = state_vals.shape[1] // 2
    block_count = row_count // CH
    step_size = jax.nn.softplus(step_raw + step_bias[None, :]) * live_mask[:, None]
    log_rates = step_size * (-jnp.exp(decay_log))[None, :]
    heads_view = conv_vals.reshape(row_count, head_count, head_size)
    values = heads_view * step_size[:, :, None]
    values = values.reshape(block_count, CH, head_count, head_size).transpose(0, 2, 1, 3)
    log_rates = log_rates.reshape(block_count, CH, head_count).transpose(0, 2, 1)
    b_rows = state_vals[:, :state_size].reshape(block_count, CH, state_size)
    c_rows = state_vals[:, state_size:].reshape(block_count, CH, state_size)
    start_state = jnp.zeros((head_count, state_size, head_size), jnp.float32)
    unused, results = lax.scan(
        jax.checkpoint(group_step), start_state, (values, log_rates, b_rows, c_rows)
    )
    mixed = results.transpose(0, 2, 1, 3).reshape(row_count, head_count, head_size)
    mixed = mixed + skip_gain[None, :, None] * heads_view
    return mixed.reshape(row_count, channels)


def gram(left, right):
    return lax.dot_general(
        left, right, (((0,), (0,)), ((), ())), preferred_element_type=jnp.float32
    )


def back_proj(grad_rows, weight):
    return lax.dot_general(
        grad_rows, weight, (((1,), (1,)), ((), ())), preferred_element_type=jnp.float32
    )


def rounded(value):
    return lax.optimization_barrier(value.astype(jnp.bfloat16)).astype(jnp.float32)


def body(
    hidden,
    lengths,
    norm_gain,
    z_weight,
    x_weight,
    bc_weight,
    dt_weight,
    x_kernel,
    bc_kernel,
    x_offset,
    bc_offset,
    step_bias,
    decay_log,
    skip_gain,
    gate_gain,
    out_weight,
    cotangent,
):
    row_count, model_width = hidden.shape
    parts = lax.axis_size("tensor")
    share = row_count // parts
    start = lax.axis_index("tensor") * share
    inputs = hidden.astype(jnp.float32)
    grad_out = cotangent.astype(jnp.float32)
    live_mask = (lax.iota(jnp.int32, row_count) < lengths[0]).astype(jnp.float32)
    scale = lax.rsqrt(jnp.mean(inputs * inputs, axis=1, keepdims=True) + epsilon)
    normed = (inputs * scale * norm_gain[None, :]).astype(jnp.bfloat16)
    gate_pre = jnp.dot(normed, z_weight, preferred_element_type=jnp.float32)
    conv_in = jnp.dot(normed, x_weight, preferred_element_type=jnp.float32)
    state_in = jnp.dot(normed, bc_weight, preferred_element_type=jnp.float32)
    step_raw = jnp.dot(normed, dt_weight, preferred_element_type=jnp.float32)
    conv_out, conv_pull = jax.vjp(conv_act, conv_in, x_kernel, x_offset)
    state_out, state_pull = jax.vjp(conv_act, state_in, bc_kernel, bc_offset)
    conv_low = rounded(conv_out)
    state_low = rounded(state_out)

    def local_mixer(conv_vals, state_vals, raw_steps, bias_steps, decay_logs, skip_gains):
        return mixer(
            conv_vals, state_vals, raw_steps, bias_steps, decay_logs, skip_gains, live_mask
        )

    mixed_out, mixer_pull = jax.vjp(
        local_mixer, conv_low, state_low, step_raw, step_bias, decay_log, skip_gain
    )
    sigmoid_gate = jax.nn.sigmoid(gate_pre)
    silu_gate = gate_pre * sigmoid_gate
    gated = mixed_out * silu_gate
    squares = lax.psum(jnp.sum(gated * gated, axis=1), "tensor")
    inv_norm = lax.rsqrt(squares / DI + epsilon)[:, None]
    unit_rows = gated * inv_norm
    branch_in = (unit_rows * gate_gain[None, :] * live_mask[:, None]).astype(jnp.bfloat16)
    own_inputs = lax.dynamic_slice_in_dim(inputs, start, share, 0)
    own_scale = lax.dynamic_slice_in_dim(scale, start, share, 0)
    branch = lax.psum(jnp.dot(branch_in, out_weight, preferred_element_type=jnp.float32), "tensor")
    output = (inputs + branch).astype(jnp.bfloat16)
    grad_out_weight = gram(branch_in, cotangent)
    grad_branch = back_proj(cotangent, out_weight) * live_mask[:, None]
    grad_gate_gain = jnp.sum(grad_branch * unit_rows, axis=0)
    grad_unit = grad_branch * gate_gain[None, :]
    cross = lax.psum(jnp.sum(grad_unit * unit_rows, axis=1), "tensor")
    grad_gated = inv_norm * (grad_unit - unit_rows * (cross / DI)[:, None])
    grad_mixed = grad_gated * silu_gate
    grad_gate_pre = grad_gated * mixed_out * sigmoid_gate * (1.0 + gate_pre * (1.0 - sigmoid_gate))
    (
        grad_conv_low,
        grad_state_part,
        grad_step_raw,
        grad_step_bias,
        grad_decay_log,
        grad_skip_gain,
    ) = mixer_pull(grad_mixed)
    grad_state_low = lax.psum(grad_state_part, "tensor")
    grad_conv_in, grad_x_kernel, grad_x_offset = conv_pull(grad_conv_low)
    grad_state_in, grad_bc_kernel, grad_bc_offset = state_pull(grad_state_low)
    low_gate = grad_gate_pre.astype(jnp.bfloat16)
    low_conv = grad_conv_in.astype(jnp.bfloat16)
    low_step = grad_step_raw.astype(jnp.bfloat16)
    low_state = lax.dynamic_slice_in_dim(grad_state_in, start, share, 0).astype(jnp.bfloat16)
    own_normed = lax.dynamic_slice_in_dim(normed, start, share, 0)
    grad_z_weight = gram(normed, low_gate)
    grad_x_weight = gram(normed, low_conv)
    grad_dt_weight = gram(normed, low_step)
    grad_bc_weight = gram(own_normed, low_state)
    state_back = back_proj(low_state, bc_weight)
    grad_normed = (
        back_proj(low_gate, z_weight)
        + back_proj(low_conv, x_weight)
        + back_proj(low_step, dt_weight)
    )
    own_part = lax.dynamic_slice_in_dim(grad_normed, start, share, 0) + state_back
    grad_normed = lax.dynamic_update_slice_in_dim(grad_normed, own_part, start, 0)
    grad_normed = lax.psum(grad_normed, "tensor")
    weighted = grad_normed * norm_gain[None, :]
    row_dots = jnp.sum(weighted * inputs, axis=1, keepdims=True)
    grad_hidden = (
        grad_out + scale * weighted - inputs * scale * scale * scale * row_dots / model_width
    )
    own_grad = lax.dynamic_slice_in_dim(grad_normed, start, share, 0)
    grad_norm_gain = jnp.sum(own_grad * own_inputs * own_scale, axis=0)
    (
        grad_z_weight,
        grad_x_weight,
        grad_dt_weight,
        grad_out_weight,
        grad_x_kernel,
        grad_x_offset,
        grad_step_bias,
        grad_decay_log,
        grad_skip_gain,
        grad_gate_gain,
        grad_bc_kernel,
        grad_bc_offset,
    ) = lax.psum(
        (
            grad_z_weight,
            grad_x_weight,
            grad_dt_weight,
            grad_out_weight,
            grad_x_kernel,
            grad_x_offset,
            grad_step_bias,
            grad_decay_log,
            grad_skip_gain,
            grad_gate_gain,
            grad_bc_kernel,
            grad_bc_offset,
        ),
        "dp",
    )
    grad_bc_weight, grad_norm_gain = lax.psum((grad_bc_weight, grad_norm_gain), ("dp", "tensor"))
    return (
        output,
        grad_hidden,
        grad_norm_gain,
        grad_z_weight,
        grad_x_weight,
        grad_bc_weight,
        grad_dt_weight,
        grad_x_kernel,
        grad_bc_kernel,
        grad_x_offset,
        grad_bc_offset,
        grad_step_bias,
        grad_decay_log,
        grad_skip_gain,
        grad_gate_gain,
        grad_out_weight,
    )


def solution(mesh):
    placed = (
        P("dp", None),
        P("dp"),
        P(),
        P(None, "tensor"),
        P(None, "tensor"),
        P(),
        P(None, "tensor"),
        P(None, "tensor"),
        P(),
        P("tensor"),
        P(),
        P("tensor"),
        P("tensor"),
        P("tensor"),
        P("tensor"),
        P("tensor", None),
        P("dp", None),
    )
    return jax.shard_map(
        body,
        mesh=mesh,
        in_specs=placed,
        out_specs=(
            P("dp", None),
            P("dp", None),
            P(),
            P(None, "tensor"),
            P(None, "tensor"),
            P(),
            P(None, "tensor"),
            P(None, "tensor"),
            P(),
            P("tensor"),
            P(),
            P("tensor"),
            P("tensor"),
            P("tensor"),
            P("tensor"),
            P("tensor", None),
        ),
        check_vma=False,
    )
```

profile of v0, /device:TPU:0, one launch (start us, length us, event | category | flops | bytes accessed | tf_op | source)
XLA Modules:
  0.0 1183.8 jit_solution(3214508663125442144)
XLA Ops:
  7.9 3.2 multiply_reduce_fusion.4
  15.1 4.1 multiply_convert_fusion.3
  19.2 3.4 copy.79
  22.6 4.3 copy.98
  30.6 3.2 copy.81
  41.9 111.8 %while.39 = (s32[]{:T(128)}, f32[8,128,64]{1,2,0:T(8,128)}, f32[8,8,256,64]{2,3,1,0:T(8,128)}, f32[8,8,128,64]{2,3,1,0:T(8,128)}, f32[8,8,256]{2,1,0:T(8,128)}, ...) while((s32[]{:T(128)}, f32[8,128,64]{1,2,0:T(8,128)}, ...), condition=%wide.region_4.5_spmd.clone, body=%wide.region_1.4_spmd.clone.sunk | while | flops 908396544 | bytes 5419819 | solution.py:63
  47.8 4.6 fusion.218
  61.9 4.6 fusion.218
  76.0 4.6 fusion.218
  90.1 4.6 fusion.218
  104.2 4.6 fusion.218
  118.3 4.6 fusion.218
  132.4 4.6 fusion.218
  146.5 4.6 fusion.218
  153.7 7.1 copy.92
  160.8 7.5 reshape.567
  168.4 10.3 multiply_reduce_fusion.13
  178.7 8.5 psum.133
  187.3 9.5 multiply_reduce_fusion.5
  196.7 5.8 psum.135
  202.6 11.1 multiply_reduce_fusion.6
  213.7 5.3 copy.84
  219.0 6.1 copy.99
  230.4 202.6 %while.40 = (s32[]{:T(128)}, f32[8,128,64]{1,2,0:T(8,128)S(1)}, f32[8,8,256,64]{2,3,1,0:T(8,128)}, f32[8,8,256]{2,1,0:T(8,128)}, f32[8,256,128]{2,1,0:T(8,128)},...) while((s32[]{:T(128)}, f32[8,128,64]{1,2,0:T(8,128)S(1)}, ...), condition=%wide.region_22.23_spmd.clone, body=%wide.region_10.22_spmd.clone.sunk | while | flops 2122338304 | bytes 16312063 | solution.py:63
  239.3 2.8 fusion.240
  248.2 3.8 fusion.243
  264.6 2.8 fusion.240
  273.5 3.8 fusion.243
  298.8 3.8 fusion.243
  324.1 3.8 fusion.243
  340.6 2.8 fusion.240
  349.5 3.8 fusion.243
  365.8 2.8 fusion.240
  374.7 3.8 fusion.243
  391.1 2.8 fusion.240
  400.0 3.8 fusion.243
  425.3 3.8 fusion.243
  433.0 3.1 pad_add_fusion.3
  436.6 8.0 fusion.107
  444.6 7.0 copy.93
  451.6 7.6 reshape.568
  461.6 5.4 copy.89
  466.9 3.2 copy.97
  474.8 7.0 multiply_reduce_fusion.10
  481.8 6.6 broadcast_multiply_fusion
  488.4 8.1 fusion.85
  496.6 5.6 fusion.124
  502.2 5.6 fusion.123
  508.0 10.3 add_add_fusion
  518.4 6.1 multiply_reduce_fusion.17
  526.2 3.4 add_dynamic-update-slice_fusion
  530.0 6.7 fusion.126
  536.7 3.9 fusion.106
  543.3 5.9 fusion.125
  550.0 6.6 convert_element_type.48
  556.9 2.9 fusion.101
  559.8 38.5 %all-reduce.22 = (f32[1024,8]{0,1:T(8,128)}, f32[4,512]{1,0:T(4,128)}, f32[4,256]{1,0:T(4,128)}, f32[512]{0:T(512)}, f32[256]{0:T(256)}, /*index=5*/f32[8]{0:T(128)}, f32[8]{0:T(128)}, f32[8]{0:T(128)}, f32[512]{0:T(512)}) all-reduce(f32[1024,8]{0,1:T(8,128)S(1)} %fusion.101, ...), channel_id=1, replica_groups=mesh['dp'=8,'tensor'=4] {'dp'}, use_global_device_ids=true, to_apply=%region_32.33 | all-reduce | flops 12568 | bytes 100544 | tf_op jit(solution)/shard_map/psum | solution.py:200
  598.2 220.3 %all-reduce.36.cloned.1.call-done = (f32[2048,1024]{1,0:T(8,128)}, f32[2048,1024]{1,0:T(8,128)}) async-done(((f32[2048,1024]{1,0:T(8,128)}, f32[2048,1024]{1,0:T(8,128)}), (f32[2048,1024]{1,0:T(8,128)}, f32[2048,1024]{1,0:T(8,128)})) %all-reduce.36.cloned.1.call-update) | async-done | bytes 16777232 | tf_op jit(solution)/shard_map/psum | solution.py:141
  821.0 39.7 %psum.138 = f32[1024]{0:T(1024)} all-reduce(f32[1024]{0:T(1024)S(1)} %multiply_reduce_fusion.18), channel_id=1, replica_groups=mesh['dp'=8,'tensor'=4] {'dp','tensor'}, use_global_device_ids=true, to_apply=%region_28.29 | all-reduce | flops 1024 | bytes 8192 | tf_op jit(solution)/shard_map/psum | solution.py:217
  860.8 6.0 multiply_reduce_fusion.3
  869.1 9.5 multiply_subtract_fusion
  878.6 76.7 %all-reduce.32.cloned.1.call-done = f32[1024,256]{1,0:T(8,128)} async-done(((f32[1024,256]{1,0:T(8,128)}), f32[1024,256]{1,0:T(8,128)}) %all-reduce.32.cloned.1.call-update) | async-done | bytes 1048592 | tf_op jit(solution)/shard_map/psum | solution.py:217
  955.3 214.6 %all-reduce.34.cloned.1.call-done = (f32[1024,512]{1,0:T(8,128)}, f32[1024,512]{1,0:T(8,128)}, f32[512,1024]{1,0:T(8,128)}) async-done(((f32[1024,512]{1,0:T(8,128)}, f32[1024,512]{1,0:T(8,128)}, f32[512,1024]{1,0:T(8,128)}), (f32[1024,512]{1,0:T(8,128)}, f32[1024,512]{1,0:T(8,128)}, f32[512,1024]{1,0:T(8,128)})) %all-reduce.34.cloned.1.call-update) | async-done | bytes 6291472 | tf_op jit(solution)/shard_map/psum | solution.py:200
  1170.0 3.2 copy.155
  (548 shorter events, 275.4 us)
Async XLA Ops:
  7.2 161.2 %copy-start = (bf16[1024,512]{1,0:T(8,128)(2,1)S(1)}, bf16[1024,512]{1,0:T(8,128)(2,1)}, u32[]{:S(2)}) copy-start(bf16[1024,512]{1,0:T(8,128)(2,1)} %param.24) | copy-start | bytes 3145732
  7.2 4.0 copy-start.54
  7.2 4.0 copy-start.32
  7.2 511.1 %all-reduce.30.cloned.1.call-start = ((), (), s32[]{:S(2)}) async-start(), calls=%async_computation | async-start | bytes 4194304 | tf_op jit(solution)/shard_map/psum | solution.py:159
  7.9 3.4 copy-start.3
  11.4 3.7 copy-start.35
  11.4 3.7 copy-start.37
  11.4 3.7 copy-start.39
  12.6 2.4 copy-start.1
  12.6 2.5 copy-start.58
  15.1 4.1 copy-start.10
  22.6 5.0 copy-start.65
  22.6 5.0 copy-start.2
  22.6 5.0 copy-start.30
  22.6 5.0 copy-start.60
  27.7 2.9 copy-start.55
  30.6 3.2 copy-start.23
  35.1 4.2 copy-start.14
  35.1 4.2 copy-start.41
  35.2 4.2 copy-start.43
  35.2 4.2 copy-start.45
  35.2 4.2 copy-start.47
  37.8 4.0 copy-start.29
  160.8 7.5 copy-start.62
  168.4 18.8 %copy-start.34 = (f32[512]{0:T(512)S(1)}, f32[512]{0:T(512)}, u32[]{:S(2)}) copy-start(f32[512]{0:T(512)} %param.35) | copy-start | bytes 6148
  225.1 5.3 copy-start.15
  433.0 3.6 copy-start.21
  436.1 382.4 %all-reduce.36.cloned.1.call-start = ((), (), s32[]{:S(2)}) async-start(), calls=%async_computation.3 | async-start | bytes 33554432 | tf_op jit(solution)/shard_map/psum | solution.py:141
  451.6 7.6 copy-start.20
  466.9 3.9 copy-start.6
  466.9 5.3 copy-start.11
  470.8 2.8 copy-start.7
  470.8 4.0 copy-start.9
  474.8 7.0 copy-start.36
  474.8 7.0 copy-start.38
  474.8 7.0 copy-start.40
  488.4 8.1 copy-start.64
  496.6 5.6 copy-start.13
  496.6 5.6 copy-start.12
  502.2 5.6 copy-start.25
  502.2 5.6 copy-start.26
  502.2 5.6 copy-start.56
  502.2 5.8 copy-start.31
  518.3 6.2 copy-start.42
  518.3 6.2 copy-start.44
  518.3 6.2 copy-start.46
  518.3 6.2 copy-start.48
  529.7 425.6 %all-reduce.32.cloned.1.call-start = ((), (), s32[]{:S(2)}) async-start(), calls=%async_computation.1 | async-start | bytes 2097152 | tf_op jit(solution)/shard_map/psum | solution.py:217
  529.9 6.7 copy-start.8
  530.0 6.7 copy-start.16
  543.3 626.7 %all-reduce.34.cloned.1.call-start = ((), (), s32[]{:S(2)}) async-start(), calls=%async_computation.2 | async-start | bytes 12582912 | tf_op jit(solution)/shard_map/psum | solution.py:200
  550.0 6.6 copy-start.49
  550.0 6.8 copy-start.50
  550.0 6.8 copy-start.51
  550.0 6.8 copy-start.52
  550.0 6.9 copy-start.53
  550.0 6.9 copy-start.66
  556.6 3.2 copy-start.59
  556.9 303.9 %copy-start.33 = (f32[1024]{0:T(1024)S(1)}, f32[1024]{0:T(1024)}, u32[]{:S(2)}) copy-start(f32[1024]{0:T(1024)} %param.23) | copy-start | bytes 12292
  860.8 6.0 copy-start.4
  860.8 8.4 copy-start.5
  1170.0 3.2 copy-start.18
  1170.0 4.6 copy-start.22
  1173.2 2.5 copy-start.17
  (7 other events, 7.7 us)
Sparse Core Ops, SparseCore 0:
  436.3 51.7 all-reduce.29
  529.8 288.6 all-reduce.35
  824.3 131.0 all-reduce.31
  960.6 209.3 all-reduce.33
where the time goes:
time: 1190 us; the launch traced here: 1180 us
  waiting for transfers between devices  512 us (43%)
  matrix products  276 us (23%)
  local copies, waits for them, and re-layouts  150 us (13%)
  other arithmetic  136 us (11%)
  blocking collectives  92.5 us (8%)
  between operations  15.4 us (1%)
    psum x1, waiting for transfers between devices, body(): lax.psum(jnp.dot(branch_in, out_weight, preferred_element_type=jnp.float3...  220 us
    psum x1, waiting for transfers between devices, body(): lax.psum((grad_z_weight, grad_x_weight, grad_dt_weight, grad_out_weight,...  215 us
    dot_general x24, matrix products, group_step(): jnp.einsum('hts,hsp->htp', scores[None] * decays, values, precision=precise)  89.6 us
    psum x1, waiting for transfers between devices, body(): lax.psum((grad_bc_weight, grad_norm_gain), ('dp', 'tensor'))  76.7 us
    psum x1, blocking collectives, body(): lax.psum((grad_bc_weight, grad_norm_gain), ('dp', 'tensor'))  39.7 us
    another operation x57, other arithmetic  38.8 us
    psum x1, blocking collectives, body(): lax.psum((grad_z_weight, grad_x_weight, grad_dt_weight, grad_out_weight,...  38.5 us
    dot_general x24, matrix products, group_step(): jnp.einsum('sn,hsp->hnp', b_rows, values * remain[:, :, None], precision=...  37.8 us
  transfers between devices with their start and end apart: 4, of which 3 were waited for; matrix products, arithmetic and copies ran while one was open for 11% of the time, Pallas kernels for 0%

commit v1 on v0

--- a/solution.py
+++ b/solution.py
@@ -138,7 +138,12 @@
     branch_in = (unit_rows * gate_gain[None, :] * live_mask[:, None]).astype(jnp.bfloat16)
     own_inputs = lax.dynamic_slice_in_dim(inputs, start, share, 0)
     own_scale = lax.dynamic_slice_in_dim(scale, start, share, 0)
-    branch = lax.psum(jnp.dot(branch_in, out_weight, preferred_element_type=jnp.float32), "tensor")
+    branch = jnp.sum(
+        lax.all_gather(
+            jnp.dot(branch_in, out_weight, preferred_element_type=jnp.float32), "tensor"
+        ),
+        axis=0,
+    )
     output = (inputs + branch).astype(jnp.bfloat16)
     grad_out_weight = gram(branch_in, cotangent)
     grad_branch = back_proj(cotangent, out_weight) * live_mask[:, None]

time: 1190 us -> 1250 us (1.050)
  waiting for transfers between devices: 512 us -> 550 us
  other arithmetic: 136 us -> 158 us
    all_gather x0 -> x1, waiting for transfers between devices: none -> 155 us  [body(): lax.all_gather(jnp.dot(branch_in, out_weight, preferred_element_type=jnp....]
    psum x1, waiting for transfers between devices: 220 us -> 76.3 us  [body(): grad_normed = lax.psum(grad_normed, 'tensor')]
    psum x1, waiting for transfers between devices: 76.7 us -> 105 us  [body(): lax.psum((grad_bc_weight, grad_norm_gain), ('dp', 'tensor'))]
    reduce_sum x0 -> x1, other arithmetic: none -> 16.7 us  [body(): jnp.sum(lax.all_gather(jnp.dot(branch_in, out_weight, preferred_element_t...]
    unnamed x141 -> x135, local copies, waits for them, and re-layouts: 29.3 us -> 26.6 us
  transfers between devices with their start and end apart: 4 -> 5, of which waited for: 3 -> 4; matrix products, arithmetic and copies ran while one was open for 11% -> 12% of each run, Pallas kernels for 0% -> 0%
where the time goes in v1:
time: 1250 us; the launch traced here: 1240 us
  waiting for transfers between devices  550 us (44%)
  matrix products  277 us (22%)
  other arithmetic  158 us (13%)
  local copies, waits for them, and re-layouts  148 us (12%)
  blocking collectives  93.4 us (7%)
  between operations  15.6 us (1%)
    psum x1, waiting for transfers between devices, body(): lax.psum((grad_z_weight, grad_x_weight, grad_dt_weight, grad_out_weight,...  215 us
    all_gather x1, waiting for transfers between devices, body(): lax.all_gather(jnp.dot(branch_in, out_weight, preferred_element_type=jnp....  155 us
    psum x1, waiting for transfers between devices, body(): lax.psum((grad_bc_weight, grad_norm_gain), ('dp', 'tensor'))  105 us
    dot_general x24, matrix products, group_step(): jnp.einsum('hts,hsp->htp', scores[None] * decays, values, precision=precise)  89.9 us
    psum x1, waiting for transfers between devices, body(): grad_normed = lax.psum(grad_normed, 'tensor')  76.3 us
    psum x1, blocking collectives, body(): lax.psum((grad_bc_weight, grad_norm_gain), ('dp', 'tensor'))  40.3 us
    another operation x57, other arithmetic  38.9 us
    psum x1, blocking collectives, body(): lax.psum((grad_z_weight, grad_x_weight, grad_dt_weight, grad_out_weight,...  38.7 us
  transfers between devices with their start and end apart: 5, of which 4 were waited for; matrix products, arithmetic and copies ran while one was open for 12% of the time, Pallas kernels for 0%

profile of v1, /device:TPU:0, one launch (start us, length us, event | category | flops | bytes accessed | tf_op | source)
XLA Modules:
  0.0 1244.3 jit_solution(1133785539458134213)
XLA Ops:
  7.9 3.2 multiply_reduce_fusion.4
  15.1 4.0 multiply_convert_fusion.3
  19.1 3.4 copy.79
  22.6 4.3 copy.98
  30.6 3.3 copy.81
  41.9 112.0 %while.39 = (s32[]{:T(128)}, f32[8,128,64]{1,2,0:T(8,128)}, f32[8,8,256,64]{2,3,1,0:T(8,128)}, f32[8,8,128,64]{2,3,1,0:T(8,128)}, f32[8,8,256]{2,1,0:T(8,128)}, ...) while((s32[]{:T(128)}, f32[8,128,64]{1,2,0:T(8,128)}, ...), condition=%wide.region_4.5_spmd.clone, body=%wide.region_1.4_spmd.clone.sunk | while | flops 908396544 | bytes 5419819 | solution.py:63
  47.8 4.6 fusion.218
  62.0 4.7 fusion.218
  76.1 4.6 fusion.218
  90.2 4.6 fusion.218
  104.3 4.6 fusion.218
  118.5 4.6 fusion.218
  132.6 4.6 fusion.218
  146.7 4.6 fusion.218
  153.9 7.1 copy.92
  161.0 7.5 reshape.568
  168.6 10.3 multiply_reduce_fusion.13
  179.0 8.5 psum.126
  187.5 9.5 multiply_reduce_fusion.5
  197.0 5.8 psum.127
  202.8 11.1 multiply_reduce_fusion.6
  213.9 5.3 copy.84
  219.3 6.1 copy.99
  230.6 203.3 %while.40 = (s32[]{:T(128)}, f32[8,128,64]{1,2,0:T(8,128)S(1)}, f32[8,8,256,64]{2,3,1,0:T(8,128)}, f32[8,8,256]{2,1,0:T(8,128)}, f32[8,256,128]{2,1,0:T(8,128)},...) while((s32[]{:T(128)}, f32[8,128,64]{1,2,0:T(8,128)S(1)}, ...), condition=%wide.region_22.23_spmd.clone, body=%wide.region_10.22_spmd.clone.sunk | while | flops 2122338304 | bytes 16312063 | solution.py:63
  248.7 3.8 fusion.243
  265.1 2.8 fusion.240
  274.1 3.8 fusion.243
  299.4 3.8 fusion.243
  324.8 3.8 fusion.243
  350.2 3.8 fusion.243
  366.6 2.8 fusion.240
  375.5 3.8 fusion.243
  391.9 2.8 fusion.240
  400.8 3.8 fusion.243
  426.2 3.8 fusion.243
  433.9 3.0 pad_add_fusion.3
  437.0 7.1 copy.93
  444.1 7.5 reshape.569
  454.2 5.4 copy.89
  459.6 3.0 copy.97
  467.0 7.0 multiply_reduce_fusion.10
  474.0 6.6 broadcast_multiply_fusion
  480.6 8.2 fusion.85
  488.8 5.6 fusion.124
  494.5 5.8 fusion.123
  500.5 10.5 add_add_fusion
  510.9 6.1 multiply_reduce_fusion.17
  518.8 3.4 add_dynamic-update-slice_fusion
  522.4 8.2 fusion.107
  530.7 6.7 fusion.126
  537.4 3.9 fusion.106
  544.1 5.9 fusion.125
  550.8 6.6 convert_element_type.48
  557.6 2.9 fusion.101
  560.5 38.7 %all-reduce.22 = (f32[1024,8]{0,1:T(8,128)}, f32[4,512]{1,0:T(4,128)}, f32[4,256]{1,0:T(4,128)}, f32[512]{0:T(512)}, f32[256]{0:T(256)}, /*index=5*/f32[8]{0:T(128)}, f32[8]{0:T(128)}, f32[8]{0:T(128)}, f32[512]{0:T(512)}) all-reduce(f32[1024,8]{0,1:T(8,128)S(1)} %fusion.101, ...), channel_id=1, replica_groups=mesh['dp'=8,'tensor'=4] {'dp'}, use_global_device_ids=true, to_apply=%region_32.33 | all-reduce | flops 12568 | bytes 100544 | tf_op jit(solution)/shard_map/psum | solution.py:205
  599.2 76.3 %all-reduce.31.cloned.1.call-done = f32[2048,1024]{1,0:T(8,128)} async-done(((f32[2048,1024]{1,0:T(8,128)}), f32[2048,1024]{1,0:T(8,128)}) %all-reduce.31.cloned.1.call-update) | async-done | bytes 8388624 | tf_op jit(solution)/shard_map/psum | solution.py:184
  678.0 40.3 %psum.130 = f32[1024]{0:T(1024)} all-reduce(f32[1024]{0:T(1024)S(1)} %multiply_reduce_fusion.18), channel_id=1, replica_groups=mesh['dp'=8,'tensor'=4] {'dp','tensor'}, use_global_device_ids=true, to_apply=%region_28.29 | all-reduce | flops 1024 | bytes 8192 | tf_op jit(solution)/shard_map/psum | solution.py:222
  718.3 6.2 multiply_reduce_fusion.3
  724.5 154.9 %all-gather.3.cloned.1.call-done = f32[8192,1024]{1,0:T(8,128)} async-done(((f32[2048,1024]{1,0:T(8,128)}), f32[8192,1024]{1,0:T(8,128)}) %all-gather.3.cloned.1.call-update) | async-done | bytes 33554448 | tf_op jit(solution)/shard_map/all_gather | solution.py:142
  879.4 16.7 %reduce_sum.387 = f32[2048,1024]{1,0:T(8,128)} reduce(f32[4,2048,1024]{2,1,0:T(8,128)} %bitcast.308, f32[]{:T(128)} %constant.134.clone.1), dimensions={0}, to_apply=%region_7.8 | reduce | flops 6291456 | bytes 41943044 | tf_op jit(solution)/shard_map/reduce_sum | solution.py:141
  896.2 15.0 %multiply_subtract_fusion = (f32[2048,1024]{1,0:T(8,128)}, bf16[2048,1024]{1,0:T(8,128)(2,1)}) fusion(bf16[2048,1024]{1,0:T(8,128)(2,1)} %param.37, bf16[2048,1024]{1,0:T(8,128)(2,1)} %param.21, f32[2048,1024]{1,0:T(8,128)} %all-reduce.31.cloned.1.call-done, f32[2048]{0:T(1024)S(1)} %multiply_reduce_fusion.3, f32[1024]{0:T(1024)S(1)} %copy-done.30, ...), kind=kLoop, calls=%fused_computation.108 | loop fusion | flops 27262976 | bytes 37769216 | tf_op jit(solution)/shard_map/sub | solution.py:188
  911.2 104.5 %all-reduce.33.cloned.1.call-done = f32[1024,256]{1,0:T(8,128)} async-done(((f32[1024,256]{1,0:T(8,128)}), f32[1024,256]{1,0:T(8,128)}) %all-reduce.33.cloned.1.call-update) | async-done | bytes 1048592 | tf_op jit(solution)/shard_map/psum | solution.py:222
  1015.7 214.6 %all-reduce.35.cloned.1.call-done = (f32[1024,512]{1,0:T(8,128)}, f32[1024,512]{1,0:T(8,128)}, f32[512,1024]{1,0:T(8,128)}) async-done(((f32[1024,512]{1,0:T(8,128)}, f32[1024,512]{1,0:T(8,128)}, f32[512,1024]{1,0:T(8,128)}), (f32[1024,512]{1,0:T(8,128)}, f32[1024,512]{1,0:T(8,128)}, f32[512,1024]{1,0:T(8,128)})) %all-reduce.35.cloned.1.call-update) | async-done | bytes 6291472 | tf_op jit(solution)/shard_map/psum | solution.py:205
  1230.3 3.2 copy.155
  (546 shorter events, 278.4 us)
Async XLA Ops:
  7.2 161.4 %copy-start = (bf16[1024,512]{1,0:T(8,128)(2,1)S(1)}, bf16[1024,512]{1,0:T(8,128)(2,1)}, u32[]{:S(2)}) copy-start(bf16[1024,512]{1,0:T(8,128)(2,1)} %param.24) | copy-start | bytes 3145732
  7.2 4.0 copy-start.51
  7.2 4.0 copy-start.29
  7.2 503.7 %all-reduce.29.cloned.1.call-start = ((), (), s32[]{:S(2)}) async-start(), calls=%async_computation | async-start | bytes 4194304 | tf_op jit(solution)/shard_map/psum | solution.py:164
  7.9 3.4 copy-start.3
  11.2 1.3 copy-start.24
  11.4 3.7 copy-start.32
  11.4 3.7 copy-start.34
  11.4 3.7 copy-start.36
  12.6 2.4 copy-start.1
  12.6 2.5 copy-start.55
  15.1 4.1 copy-start.8
  22.6 5.0 copy-start.62
  22.6 5.0 copy-start.2
  22.6 5.0 copy-start.27
  22.6 5.0 copy-start.57
  27.6 2.9 copy-start.52
  30.5 3.3 copy-start.20
  33.8 1.4 copy-start.58
  35.1 4.2 copy-start.12
  35.2 4.2 copy-start.38
  35.2 4.2 copy-start.40
  35.2 4.2 copy-start.42
  35.2 4.2 copy-start.44
  37.9 4.0 copy-start.26
  161.0 7.5 copy-start.59
  168.6 18.9 %copy-start.31 = (f32[512]{0:T(512)S(1)}, f32[512]{0:T(512)}, u32[]{:S(2)}) copy-start(f32[512]{0:T(512)} %param.35) | copy-start | bytes 6148
  225.4 5.2 copy-start.13
  437.0 238.5 %all-reduce.31.cloned.1.call-start = ((), (), s32[]{:S(2)}) async-start(), calls=%async_computation.1 | async-start | bytes 16777216 | tf_op jit(solution)/shard_map/psum | solution.py:184
  444.1 7.6 copy-start.18
  459.6 3.5 copy-start.4
  459.6 4.9 copy-start.9
  463.1 2.7 copy-start.5
  463.1 3.9 copy-start.7
  467.0 7.0 copy-start.33
  467.0 7.0 copy-start.35
  467.0 7.0 copy-start.37
  480.6 8.2 copy-start.61
  488.8 5.6 copy-start.11
  488.8 5.6 copy-start.10
  494.4 5.8 copy-start.22
  494.4 5.8 copy-start.23
  494.4 5.8 copy-start.53
  494.5 6.0 copy-start.28
  510.9 6.1 copy-start.39
  510.9 6.1 copy-start.41
  510.9 6.1 copy-start.43
  510.9 6.1 copy-start.45
  522.2 357.2 %all-gather.3.cloned.1.call-start = ((), (), s32[]{:S(2)}) async-start(), calls=%async_computation.3 | async-start | bytes 41943040 | tf_op jit(solution)/shard_map/all_gather | solution.py:142
  530.6 485.1 %all-reduce.33.cloned.1.call-start = ((), (), s32[]{:S(2)}) async-start(), calls=%async_computation.2 | async-start | bytes 2097152 | tf_op jit(solution)/shard_map/psum | solution.py:222
  530.7 6.7 copy-start.6
  530.7 6.7 copy-start.14
  544.0 686.3 %all-reduce.35.cloned.1.call-start = ((), (), s32[]{:S(2)}) async-start(), calls=%async_computation.4 | async-start | bytes 12582912 | tf_op jit(solution)/shard_map/psum | solution.py:205
  550.8 6.6 copy-start.46
  550.8 6.8 copy-start.47
  550.8 6.8 copy-start.48
  550.8 6.8 copy-start.49
  550.8 6.8 copy-start.50
  550.8 6.8 copy-start.63
  557.3 3.2 copy-start.56
  557.6 160.7 %copy-start.30 = (f32[1024]{0:T(1024)S(1)}, f32[1024]{0:T(1024)}, u32[]{:S(2)}) copy-start(f32[1024]{0:T(1024)} %param.23) | copy-start | bytes 12292
  1230.3 3.2 copy-start.16
  1230.3 4.6 copy-start.19
  1233.6 2.5 copy-start.15
  (5 other events, 4.9 us)
Sparse Core Ops, SparseCore 0:
  437.1 51.7 all-reduce.28
  522.3 153.1 all-reduce.30
  677.0 202.3 all-gather.2
  885.0 130.6 all-reduce.32
  1021.0 209.3 all-reduce.34
